TPU v7x, 32 devices: a whole 2x2x4 slice. The times are simulated.
32 devices in a mesh: gx: 8 (over z, x), gy: 4 (over y, core).
Axes of the slice: x: 2, y: 2, z: 4, core: 2. Of those that a mesh axis runs over, the one named last changes fastest.
Arguments:
- prior_basis: float32 [128, 128, 128], P('gx', 'gy'), may hold values from -6 to 6
- cond_x: float32 [128, 128], P('gx', 'gy'), may hold values from 0.5 to 5
- cond_y: float32 [128, 128], P('gx', 'gy'), may hold values from 0.5 to 5
- capacitance: float32 [128, 128], P('gx', 'gy'), may hold values from 0.05 to 1
- pad_mask: int32 [128, 128], P('gx', 'gy'), may hold values 0 or 1
- port_nodes: int32 [128], replicated, may hold values from 0 to 16383
Outputs:
- new_basis: float32 [128, 128, 128], P('gx', 'gy')
- reduced_g: float32 [128, 128], replicated
- reduced_c: float32 [128, 128], replicated
Inputs may be any that keep to these rules, and one draw needn't show every extreme that they name: `port_nodes`: a row-major node index into the grid of 128 x 128 nodes.
All inputs are finite; a program needn't handle non-finite values. No bound on the sum of `pad_mask` on one device may be relied on, other than what follows from the above.
Results may differ from a plain program's by a relative error of at most 0.0003.
Values sent between devices are 32-bit elements; how exact they have to be, the bound alone decides.
No kernel may reach another device: no remote copies, remote signals or barrier semaphores. Data moves between devices by JAX's collectives and lax.ppermute only.
A program may use at most 64 MiB of HBM per device.

v0:
```python
import jax
import jax.numpy as jnp
from jax import lax
from jax.sharding import PartitionSpec as P

SWEEPS = 4
shift_point = 0.5
supply_conductance = 4.0
port_current = 8.0
highest = lax.Precision.HIGHEST


def shifted(shard, axis, by):
    devices = lax.axis_size(axis)
    pairs = [(i, i + by) for i in range(devices) if 0 <= i + by < devices]
    return lax.ppermute(shard, axis, pairs)


def padded(cells, sides, width):
    for axis, dim in sides:
        count = lax.axis_size(axis)
        ends = count - 1
        head = lax.slice_in_dim(cells, 0, width, axis=dim)
        tail = lax.slice_in_dim(cells, cells.shape[dim] - width, cells.shape[dim], axis=dim)
        cells = jnp.concatenate(
            [
                lax.ppermute(tail, axis, [(i, (i + 1) % count) for i in range(ends)]),
                cells,
                lax.ppermute(head, axis, [((i + 1) % count, i) for i in range(ends)]),
            ],
            axis=dim,
        )
    return cells


def neighbors(ext, links):
    cx, cy, cx_up, cy_left = links
    total = cx[:, :, None] * ext[2:, 1:-1] + cx_up[:, :, None] * ext[:-2, 1:-1]
    return total + cy[:, :, None] * ext[1:-1, 2:] + cy_left[:, :, None] * ext[1:-1, :-2]


def local_inner(left, right):
    a = left.reshape(-1, left.shape[-1])
    b = right.reshape(-1, right.shape[-1])
    return jnp.einsum("cp,cq->pq", a, b, precision=highest, preferred_element_type=jnp.float32)


def per_device(prior_basis, cond_x, cond_y, capacitance, pad_mask, port_nodes):
    rows_dev, cols_dev = cond_x.shape
    width = port_nodes.shape[0]
    count_x = lax.axis_size("gx")
    count_y = lax.axis_size("gy")
    total_rows = rows_dev * count_x
    total_cols = cols_dev * count_y
    nodes = total_rows * total_cols
    row_start = lax.axis_index("gx") * rows_dev
    col_start = lax.axis_index("gy") * cols_dev
    global_rows = row_start + jnp.arange(rows_dev, dtype=jnp.int32)[:, None]
    global_cols = col_start + jnp.arange(cols_dev, dtype=jnp.int32)[None, :]
    cx = jnp.where(global_rows < total_rows - 1, cond_x, jnp.float32(0.0))
    cy = jnp.where(global_cols < total_cols - 1, cond_y, jnp.float32(0.0))
    above = shifted(cx[-1:, :], "gx", 1)
    beside = shifted(cy[:, -1:], "gy", 1)
    cx_up = jnp.concatenate([above, cx[:-1]], axis=0)
    cy_left = jnp.concatenate([beside, cy[:, :-1]], axis=1)
    links = (cx, cy, cx_up, cy_left)
    diag_g = cx + cx_up + cy + cy_left + supply_conductance * pad_mask.astype(jnp.float32)
    diag = (diag_g + shift_point * capacitance)[:, :, None]
    node_ids = global_rows * total_cols + global_cols
    onehot = (node_ids[:, :, None] == port_nodes[None, None, :]).astype(jnp.float32)
    rhs = capacitance[:, :, None] * prior_basis + port_current * onehot

    def sweep(step, current):
        ext = padded(current, (("gx", 0), ("gy", 1)), 1)
        return (rhs + neighbors(ext, links)) / diag

    field = lax.fori_loop(0, SWEEPS, sweep, rhs / diag)
    proj = lax.psum(local_inner(prior_basis, field), ("gx", "gy")) / nodes
    cand = field - jnp.einsum("xyk,kp->xyp", prior_basis, proj, precision=highest)
    gram = lax.psum(local_inner(cand, cand), ("gx", "gy")) / nodes
    lower = jnp.linalg.cholesky(gram)
    flat = cand.reshape(-1, width)
    basis_flat = lax.linalg.triangular_solve(
        lower, flat, left_side=False, lower=True, transpose_a=True
    )
    new_basis = basis_flat.reshape(rows_dev, cols_dev, width)
    ext = padded(new_basis, (("gx", 0), ("gy", 1)), 1)
    g_image = diag_g[:, :, None] * new_basis - neighbors(ext, links)
    g_raw, c_raw = lax.psum(
        (
            local_inner(new_basis, g_image),
            local_inner(new_basis, capacitance[:, :, None] * new_basis),
        ),
        ("gx", "gy"),
    )
    reduced_g = g_raw / nodes
    reduced_c = c_raw / nodes
    return (new_basis, reduced_g, reduced_c)


def solution(mesh):
    placed = (P("gx", "gy", None), P("gx", "gy"), P("gx", "gy"), P("gx", "gy"), P("gx", "gy"), P())
    return jax.shard_map(
        per_device,
        mesh=mesh,
        in_specs=placed,
        out_specs=(P("gx", "gy", None), P(), P()),
        check_vma=False,
    )
```

profile of v0, /device:TPU:0, one launch (start us, length us, event | category | flops | bytes accessed | tf_op | source)
XLA Modules:
  0.0 506.1 jit_solution(9967310550308028480)
XLA Ops:
  7.9 2.5 collective-permute-start.5
  10.5 4.2 collective-permute-start.4
  18.0 68.9 %while.10 = (s32[]{:T(128)}, f32[16,32,128]{2,1,0:T(8,128)S(1)}, f32[16,32]{1,0:T(8,128)S(1)}, f32[16,32]{1,0:T(8,128)S(1)}, f32[16,32]{1,0:T(8,128)S(1)}, /*ind...) while((s32[]{:T(128)}, f32[16,32,128]{2,1,0:T(8,128)S(1)}, ...), condition=%wide.region_1.2_spmd, body=%wide.region_0.1_spmd.sunk | while | flops 851970 | bytes 2564349 | solution.py:77
  18.1 4.3 collective-permute-start
  23.8 4.6 collective-permute-done.1
  31.2 3.6 collective-permute-done.3
  35.2 4.8 collective-permute-start
  41.5 4.2 collective-permute-done.1
  45.7 2.9 collective-permute-start.2
  49.9 2.7 collective-permute-done.3
  53.1 2.9 collective-permute-start
  57.5 4.2 collective-permute-done.1
  61.7 3.2 collective-permute-start.2
  69.1 4.8 collective-permute-start
  75.4 4.2 collective-permute-done.1
  79.6 2.9 collective-permute-start.2
  83.8 2.7 collective-permute-done.3
  88.3 117.4 %all-reduce.5.cloned.1.call-done = f32[128,128]{0,1:T(8,128)} async-done(((f32[128,128]{0,1:T(8,128)}), f32[128,128]{0,1:T(8,128)}) %all-reduce.5.cloned.1.call-update) | async-done | bytes 65552 | tf_op jit(solution)/shard_map/psum | solution.py:78
  208.2 122.0 %all-reduce.7.cloned.1.call-done = f32[128,128]{0,1:T(8,128)} async-done(((f32[128,128]{0,1:T(8,128)}), f32[128,128]{0,1:T(8,128)}) %all-reduce.7.cloned.1.call-update) | async-done | bytes 65552 | tf_op jit(solution)/shard_map/psum | solution.py:80
  331.9 11.7 %cholesky.16 = f32[128,128]{1,0:T(8,128)S(1)} custom-call(f32[128,128]{1,0:T(8,128)S(1)} %fusion.24), custom_call_target="Cholesky" | custom-call | tf_op jit(solution)/shard_map/jit(cholesky)/cholesky | solution.py:81
  345.0 9.8 %custom-call.6 = f32[1,128,128]{1,2,0:T(8,128)S(1)} custom-call(f32[1,128,128]{2,1,0:T(8,128)S(1)} %fusion.21), custom_call_target="InvertDiagBlocksLowerTriangular" | custom-call | tf_op jit(solution)/shard_map/triangular_solve | solution.py:83
  356.5 4.5 collective-permute-start.7
  363.8 3.0 collective-permute-start.9
  369.8 127.4 %all-reduce.9.cloned.1.call-done = (f32[128,128]{0,1:T(8,128)}, f32[128,128]{0,1:T(8,128)}) async-done(((f32[128,128]{0,1:T(8,128)}, f32[128,128]{0,1:T(8,128)}), (f32[128,128]{0,1:T(8,128)}, f32[128,128]{0,1:T(8,128)})) %all-reduce.9.cloned.1.call-update) | async-done | bytes 131088 | tf_op jit(solution)/shard_map/psum | solution.py:89
  (106 shorter events, 37.2 us)
Async XLA Ops:
  7.2 198.5 %all-reduce.5.cloned.1.call-start = ((), (), s32[]{:S(2)}) async-start(), calls=%async_computation | async-start | bytes 131072 | tf_op jit(solution)/shard_map/psum | solution.py:78
  7.9 6.9 %collective-permute-start.5 = (f32[16,1]{1,0:T(8,128)S(1)}, f32[16,1]{1,0:T(8,128)S(1)}, u32[]{:S(2)}, u32[]{:S(2)}) collective-permute-start(f32[16,1]{1,0:T(8,128)S(1)} %slice.102), channel_id=1, source_target_pairs={{0,1},{1,2},{2,3},{4,5},{5,6},{6,7},{8,9},{9,10},{10,11},{12,13},{... | collective-permute-start | bytes 200 | tf_op jit(solution)/shard_map/ppermute | solution.py:16
  10.5 5.5 %collective-permute-start.4 = (f32[1,32]{1,0:T(1,128)S(1)}, f32[1,32]{1,0:T(1,128)S(1)}, u32[]{:S(2)}, u32[]{:S(2)}) collective-permute-start(f32[1,32]{1,0:T(1,128)S(1)} %slice.100), channel_id=1, source_target_pairs={{0,4},{4,8},{8,12},{12,16},{16,20},{20,24},{24,28},{1,5},{5,9},{9,... | collective-permute-start | bytes 392 | tf_op jit(solution)/shard_map/ppermute | solution.py:16
  18.1 5.7 %collective-permute-start = (f32[1,32,128]{2,1,0:T(8,128)S(1)}, f32[1,32,128]{2,1,0:T(8,128)S(1)}, u32[]{:S(2)}, u32[]{:S(2)}) collective-permute-start(f32[1,32,128]{2,1,0:T(8,128)S(1)} %get-tuple-element.136), channel_id=1, source_target_pairs={{0,4},{4,8},{8,12},{12,16},{16,20},{20,24},{24,28},{1,5},{5,9},{9,... | collective-permute-start | bytes 49160 | tf_op jit(solution)/shard_map/while/body/eval_jaxpr/ppermute | solution.py:27
  22.4 6.1 %collective-permute-start.1 = (f32[1,32,128]{2,1,0:T(8,128)S(1)}, f32[1,32,128]{2,1,0:T(8,128)S(1)}, u32[]{:S(2)}, u32[]{:S(2)}) collective-permute-start(f32[1,32,128]{2,1,0:T(8,128)S(1)} %get-tuple-element.137), channel_id=1, source_target_pairs={{4,0},{8,4},{12,8},{16,12},{20,16},{24,20},{28,24},{5,1},{9,5},{13... | collective-permute-start | bytes 49160 | tf_op jit(solution)/shard_map/while/body/eval_jaxpr/ppermute | solution.py:29
  29.9 4.9 collective-permute-start.3
  35.2 6.3 %collective-permute-start = (f32[1,32,128]{2,1,0:T(8,128)S(1)}, f32[1,32,128]{2,1,0:T(8,128)S(1)}, u32[]{:S(2)}, u32[]{:S(2)}) collective-permute-start(f32[1,32,128]{2,1,0:T(8,128)S(1)} %get-tuple-element.136), channel_id=1, source_target_pairs={{0,4},{4,8},{8,12},{12,16},{16,20},{20,24},{24,28},{1,5},{5,9},{9,... | collective-permute-start | bytes 49160 | tf_op jit(solution)/shard_map/while/body/eval_jaxpr/ppermute | solution.py:27
  40.1 5.6 %collective-permute-start.1 = (f32[1,32,128]{2,1,0:T(8,128)S(1)}, f32[1,32,128]{2,1,0:T(8,128)S(1)}, u32[]{:S(2)}, u32[]{:S(2)}) collective-permute-start(f32[1,32,128]{2,1,0:T(8,128)S(1)} %get-tuple-element.137), channel_id=1, source_target_pairs={{4,0},{8,4},{12,8},{16,12},{20,16},{24,20},{28,24},{5,1},{9,5},{13... | collective-permute-start | bytes 49160 | tf_op jit(solution)/shard_map/while/body/eval_jaxpr/ppermute | solution.py:29
  45.7 4.2 collective-permute-start.2
  48.6 4.0 collective-permute-start.3
  53.1 4.4 collective-permute-start
  56.1 5.6 %collective-permute-start.1 = (f32[1,32,128]{2,1,0:T(8,128)S(1)}, f32[1,32,128]{2,1,0:T(8,128)S(1)}, u32[]{:S(2)}, u32[]{:S(2)}) collective-permute-start(f32[1,32,128]{2,1,0:T(8,128)S(1)} %get-tuple-element.137), channel_id=1, source_target_pairs={{4,0},{8,4},{12,8},{16,12},{20,16},{24,20},{28,24},{5,1},{9,5},{13... | collective-permute-start | bytes 49160 | tf_op jit(solution)/shard_map/while/body/eval_jaxpr/ppermute | solution.py:29
  61.7 4.5 collective-permute-start.2
  64.9 3.8 collective-permute-start.3
  69.1 6.3 %collective-permute-start = (f32[1,32,128]{2,1,0:T(8,128)S(1)}, f32[1,32,128]{2,1,0:T(8,128)S(1)}, u32[]{:S(2)}, u32[]{:S(2)}) collective-permute-start(f32[1,32,128]{2,1,0:T(8,128)S(1)} %get-tuple-element.136), channel_id=1, source_target_pairs={{0,4},{4,8},{8,12},{12,16},{16,20},{20,24},{24,28},{1,5},{5,9},{9,... | collective-permute-start | bytes 49160 | tf_op jit(solution)/shard_map/while/body/eval_jaxpr/ppermute | solution.py:27
  73.9 5.6 %collective-permute-start.1 = (f32[1,32,128]{2,1,0:T(8,128)S(1)}, f32[1,32,128]{2,1,0:T(8,128)S(1)}, u32[]{:S(2)}, u32[]{:S(2)}) collective-permute-start(f32[1,32,128]{2,1,0:T(8,128)S(1)} %get-tuple-element.137), channel_id=1, source_target_pairs={{4,0},{8,4},{12,8},{16,12},{20,16},{24,20},{28,24},{5,1},{9,5},{13... | collective-permute-start | bytes 49160 | tf_op jit(solution)/shard_map/while/body/eval_jaxpr/ppermute | solution.py:29
  79.6 4.2 collective-permute-start.2
  82.5 4.0 collective-permute-start.3
  88.2 242.0 %all-reduce.7.cloned.1.call-start = ((), (), s32[]{:S(2)}) async-start(), calls=%async_computation.1 | async-start | bytes 131072 | tf_op jit(solution)/shard_map/psum | solution.py:80
  208.2 289.1 %all-reduce.9.cloned.1.call-start = ((), (), s32[]{:S(2)}) async-start(), calls=%async_computation.2 | async-start | bytes 262144 | tf_op jit(solution)/shard_map/psum | solution.py:89
  355.2 5.9 %collective-permute-start.6 = (f32[1,32,128]{2,1,0:T(8,128)S(1)}, f32[1,32,128]{2,1,0:T(8,128)S(1)}, u32[]{:S(2)}, u32[]{:S(2)}) collective-permute-start(f32[1,32,128]{2,1,0:T(8,128)S(1)} %get-tuple-element.80), channel_id=1, source_target_pairs={{4,0},{8,4},{12,8},{16,12},{20,16},{24,20},{28,24},{5,1},{9,5},{13... | collective-permute-start | bytes 49160 | tf_op jit(solution)/shard_map/ppermute | solution.py:29
  356.5 6.0 %collective-permute-start.7 = (f32[1,32,128]{2,1,0:T(8,128)S(1)}, f32[1,32,128]{2,1,0:T(8,128)S(1)}, u32[]{:S(2)}, u32[]{:S(2)}) collective-permute-start(f32[1,32,128]{2,1,0:T(8,128)S(1)} %get-tuple-element.79), channel_id=1, source_target_pairs={{0,4},{4,8},{8,12},{12,16},{16,20},{20,24},{24,28},{1,5},{5,9},{9,... | collective-permute-start | bytes 49160 | tf_op jit(solution)/shard_map/ppermute | solution.py:27
  362.5 5.7 %collective-permute-start.8 = (f32[18,1,128]{2,1,0:T(1,128)S(1)}, f32[18,1,128]{2,1,0:T(1,128)S(1)}, u32[]{:S(2)}, u32[]{:S(2)}) collective-permute-start(f32[18,1,128]{2,1,0:T(1,128)S(1)} %get-tuple-element.77), channel_id=1, source_target_pairs={{1,0},{2,1},{3,2},{5,4},{6,5},{7,6},{9,8},{10,9},{11,10},{13,12},{... | collective-permute-start | bytes 27656 | tf_op jit(solution)/shard_map/ppermute | solution.py:29
  363.8 4.4 collective-permute-start.9
  (9 other events, 92.3 us)
Sparse Core Ops, SparseCore 0:
  88.3 117.3 all-reduce.4
  211.8 118.3 all-reduce.6
  369.9 127.2 all-reduce.8
where the time goes:
time: 507 us; the launch traced here: 506 us
  waiting for transfers between devices  399 us (79%)
  starting transfers between devices  54.5 us (11%)
  other arithmetic  28.1 us (6%)
  between operations  14 us (3%)
  matrix products  6.58 us (1%)
    psum x1, waiting for transfers between devices, per_device(): lax.psum((local_inner(new_basis, g_image), local_inner(new_basis, capacit...  127 us
    psum x1, waiting for transfers between devices, per_device(): gram = lax.psum(local_inner(cand, cand), ('gx', 'gy')) / nodes  122 us
    psum x1, waiting for transfers between devices, per_device(): proj = lax.psum(local_inner(prior_basis, field), ('gx', 'gy')) / nodes  117 us
    ppermute x10, starting transfers between devices, padded(): lax.ppermute(tail, axis, [(i, (i + 1) % count) for i in range(ends)])  34.8 us
    ppermute x10, waiting for transfers between devices, padded(): lax.ppermute(head, axis, [((i + 1) % count, i) for i in range(ends)])  28.7 us
    ppermute x10, starting transfers between devices, padded(): lax.ppermute(head, axis, [((i + 1) % count, i) for i in range(ends)])  12.9 us
    another operation x3, other arithmetic, per_device(): lower = jnp.linalg.cholesky(gram)  12.4 us
    another operation x2, other arithmetic, per_device(): lax.linalg.triangular_solve(lower, flat, left_side=False, lower=True, tra...  10.5 us
  transfers between devices with their start and end apart: 25, of which 17 were waited for; matrix products, arithmetic and copies ran while one was open for 0% of the time, Pallas kernels for 0%

commit v1 on v0

--- a/solution.py
+++ b/solution.py
@@ -87,11 +87,14 @@
     ext = padded(new_basis, (("gx", 0), ("gy", 1)), 1)
     g_image = diag_g[:, :, None] * new_basis - neighbors(ext, links)
     g_raw, c_raw = lax.psum(
-        (
-            local_inner(new_basis, g_image),
-            local_inner(new_basis, capacitance[:, :, None] * new_basis),
+        lax.psum(
+            (
+                local_inner(new_basis, g_image),
+                local_inner(new_basis, capacitance[:, :, None] * new_basis),
+            ),
+            "gy",
         ),
-        ("gx", "gy"),
+        "gx",
     )
     reduced_g = g_raw / nodes
     reduced_c = c_raw / nodes

time: 507 us -> 489 us (0.964)
  waiting for transfers between devices: 399 us -> 381 us
    psum x1, waiting for transfers between devices: 127 us -> 36.1 us  [per_device(): lax.psum((local_inner(new_basis, g_image), local_inner(new_basis, capacit...]
    psum x0 -> x1, waiting for transfers between devices: none -> 73.6 us  [per_device(): lax.psum(lax.psum((local_inner(new_basis, g_image), local_inner(new_basis...]
  transfers between devices with their start and end apart: 25 -> 26, of which waited for: 17 -> 18; matrix products, arithmetic and copies ran while one was open for 0% -> 0% of each run, Pallas kernels for 0% -> 0%
where the time goes in v1:
time: 489 us; the launch traced here: 488 us
  waiting for transfers between devices  381 us (78%)
  starting transfers between devices  54.6 us (11%)
  other arithmetic  28.1 us (6%)
  between operations  14 us (3%)
  matrix products  6.59 us (1%)
    psum x1, waiting for transfers between devices, per_device(): gram = lax.psum(local_inner(cand, cand), ('gx', 'gy')) / nodes  122 us
    psum x1, waiting for transfers between devices, per_device(): proj = lax.psum(local_inner(prior_basis, field), ('gx', 'gy')) / nodes  117 us
    psum x1, waiting for transfers between devices, per_device(): lax.psum(lax.psum((local_inner(new_basis, g_image), local_inner(new_basis...  73.6 us
    psum x1, waiting for transfers between devices, per_device(): lax.psum((local_inner(new_basis, g_image), local_inner(new_basis, capacit...  36.1 us
    ppermute x10, starting transfers between devices, padded(): lax.ppermute(tail, axis, [(i, (i + 1) % count) for i in range(ends)])  34.8 us
    ppermute x10, waiting for transfers between devices, padded(): lax.ppermute(head, axis, [((i + 1) % count, i) for i in range(ends)])  28.7 us
    ppermute x10, starting transfers between devices, padded(): lax.ppermute(head, axis, [((i + 1) % count, i) for i in range(ends)])  12.9 us
    another operation x3, other arithmetic, per_device(): lower = jnp.linalg.cholesky(gram)  12.4 us
  transfers between devices with their start and end apart: 26, of which 18 were waited for; matrix products, arithmetic and copies ran while one was open for 0% of the time, Pallas kernels for 0%

profile of v1, /device:TPU:0, one launch (start us, length us, event | category | flops | bytes accessed | tf_op | source)
XLA Modules:
  0.0 488.4 jit_solution(14497406423800087461)
XLA Ops:
  10.5 4.2 collective-permute-start.4
  18.0 68.9 %while.10 = (s32[]{:T(128)}, f32[16,32,128]{2,1,0:T(8,128)S(1)}, f32[16,32]{1,0:T(8,128)S(1)}, f32[16,32]{1,0:T(8,128)S(1)}, f32[16,32]{1,0:T(8,128)S(1)}, /*ind...) while((s32[]{:T(128)}, f32[16,32,128]{2,1,0:T(8,128)S(1)}, ...), condition=%wide.region_1.2_spmd, body=%wide.region_0.1_spmd.sunk | while | flops 851970 | bytes 2564349 | solution.py:77
  18.1 4.3 collective-permute-start
  23.8 4.6 collective-permute-done.1
  31.2 3.6 collective-permute-done.3
  35.2 4.8 collective-permute-start
  41.5 4.2 collective-permute-done.1
  45.7 2.9 collective-permute-start.2
  49.9 2.7 collective-permute-done.3
  53.1 2.9 collective-permute-start
  57.5 4.2 collective-permute-done.1
  61.7 3.2 collective-permute-start.2
  69.1 4.8 collective-permute-start
  75.4 4.2 collective-permute-done.1
  79.6 2.9 collective-permute-start.2
  83.8 2.7 collective-permute-done.3
  88.3 117.4 %all-reduce.7.cloned.1.call-done = f32[128,128]{0,1:T(8,128)} async-done(((f32[128,128]{0,1:T(8,128)}), f32[128,128]{0,1:T(8,128)}) %all-reduce.7.cloned.1.call-update) | async-done | bytes 65552 | tf_op jit(solution)/shard_map/psum | solution.py:78
  208.2 122.0 %all-reduce.9.cloned.1.call-done = f32[128,128]{0,1:T(8,128)} async-done(((f32[128,128]{0,1:T(8,128)}), f32[128,128]{0,1:T(8,128)}) %all-reduce.9.cloned.1.call-update) | async-done | bytes 65552 | tf_op jit(solution)/shard_map/psum | solution.py:80
  331.9 11.7 %cholesky.16 = f32[128,128]{1,0:T(8,128)S(1)} custom-call(f32[128,128]{1,0:T(8,128)S(1)} %fusion.24), custom_call_target="Cholesky" | custom-call | tf_op jit(solution)/shard_map/jit(cholesky)/cholesky | solution.py:81
  345.0 9.8 %custom-call.6 = f32[1,128,128]{1,2,0:T(8,128)S(1)} custom-call(f32[1,128,128]{2,1,0:T(8,128)S(1)} %fusion.21), custom_call_target="InvertDiagBlocksLowerTriangular" | custom-call | tf_op jit(solution)/shard_map/triangular_solve | solution.py:83
  356.5 4.5 collective-permute-start.7
  363.8 3.0 collective-permute-start.9
  369.9 36.1 %all-reduce.13.cloned.1.call-done = (f32[128,128]{0,1:T(8,128)}, f32[128,128]{0,1:T(8,128)}) async-done(((f32[128,128]{0,1:T(8,128)}, f32[128,128]{0,1:T(8,128)}), (f32[128,128]{0,1:T(8,128)}, f32[128,128]{0,1:T(8,128)})) %all-reduce.13.cloned.1.call-update) | async-done | bytes 131088 | tf_op jit(solution)/shard_map/psum | solution.py:90
  406.0 73.6 %all-reduce.11.cloned.1.call-done = (f32[128,128]{0,1:T(8,128)}, f32[128,128]{0,1:T(8,128)}) async-done(((f32[128,128]{0,1:T(8,128)}, f32[128,128]{0,1:T(8,128)}), (f32[128,128]{0,1:T(8,128)}, f32[128,128]{0,1:T(8,128)})) %all-reduce.11.cloned.1.call-update) | async-done | bytes 131088 | tf_op jit(solution)/shard_map/psum | solution.py:89
  (109 shorter events, 39.7 us)
Async XLA Ops:
  7.2 198.5 %all-reduce.7.cloned.1.call-start = ((), (), s32[]{:S(2)}) async-start(), calls=%async_computation | async-start | bytes 131072 | tf_op jit(solution)/shard_map/psum | solution.py:78
  7.9 6.9 %collective-permute-start.5 = (f32[16,1]{1,0:T(8,128)S(1)}, f32[16,1]{1,0:T(8,128)S(1)}, u32[]{:S(2)}, u32[]{:S(2)}) collective-permute-start(f32[16,1]{1,0:T(8,128)S(1)} %slice.102), channel_id=1, source_target_pairs={{0,1},{1,2},{2,3},{4,5},{5,6},{6,7},{8,9},{9,10},{10,11},{12,13},{... | collective-permute-start | bytes 200 | tf_op jit(solution)/shard_map/ppermute | solution.py:16
  10.5 5.5 %collective-permute-start.4 = (f32[1,32]{1,0:T(1,128)S(1)}, f32[1,32]{1,0:T(1,128)S(1)}, u32[]{:S(2)}, u32[]{:S(2)}) collective-permute-start(f32[1,32]{1,0:T(1,128)S(1)} %slice.100), channel_id=1, source_target_pairs={{0,4},{4,8},{8,12},{12,16},{16,20},{20,24},{24,28},{1,5},{5,9},{9,... | collective-permute-start | bytes 392 | tf_op jit(solution)/shard_map/ppermute | solution.py:16
  18.1 5.7 %collective-permute-start = (f32[1,32,128]{2,1,0:T(8,128)S(1)}, f32[1,32,128]{2,1,0:T(8,128)S(1)}, u32[]{:S(2)}, u32[]{:S(2)}) collective-permute-start(f32[1,32,128]{2,1,0:T(8,128)S(1)} %get-tuple-element.138), channel_id=1, source_target_pairs={{0,4},{4,8},{8,12},{12,16},{16,20},{20,24},{24,28},{1,5},{5,9},{9,... | collective-permute-start | bytes 49160 | tf_op jit(solution)/shard_map/while/body/eval_jaxpr/ppermute | solution.py:27
  22.4 6.1 %collective-permute-start.1 = (f32[1,32,128]{2,1,0:T(8,128)S(1)}, f32[1,32,128]{2,1,0:T(8,128)S(1)}, u32[]{:S(2)}, u32[]{:S(2)}) collective-permute-start(f32[1,32,128]{2,1,0:T(8,128)S(1)} %get-tuple-element.139), channel_id=1, source_target_pairs={{4,0},{8,4},{12,8},{16,12},{20,16},{24,20},{28,24},{5,1},{9,5},{13... | collective-permute-start | bytes 49160 | tf_op jit(solution)/shard_map/while/body/eval_jaxpr/ppermute | solution.py:29
  29.9 4.9 %collective-permute-start.3 = (f32[18,1,128]{2,1,0:T(1,128)S(1)}, f32[18,1,128]{2,1,0:T(1,128)S(1)}, u32[]{:S(2)}, u32[]{:S(2)}) collective-permute-start(f32[18,1,128]{2,1,0:T(1,128)S(1)} %get-tuple-element.141), channel_id=1, source_target_pairs={{1,0},{2,1},{3,2},{5,4},{6,5},{7,6},{9,8},{10,9},{11,10},{13,12},{... | collective-permute-start | bytes 27656 | tf_op jit(solution)/shard_map/while/body/eval_jaxpr/ppermute | solution.py:29
  35.2 6.3 %collective-permute-start = (f32[1,32,128]{2,1,0:T(8,128)S(1)}, f32[1,32,128]{2,1,0:T(8,128)S(1)}, u32[]{:S(2)}, u32[]{:S(2)}) collective-permute-start(f32[1,32,128]{2,1,0:T(8,128)S(1)} %get-tuple-element.138), channel_id=1, source_target_pairs={{0,4},{4,8},{8,12},{12,16},{16,20},{20,24},{24,28},{1,5},{5,9},{9,... | collective-permute-start | bytes 49160 | tf_op jit(solution)/shard_map/while/body/eval_jaxpr/ppermute | solution.py:27
  40.1 5.6 %collective-permute-start.1 = (f32[1,32,128]{2,1,0:T(8,128)S(1)}, f32[1,32,128]{2,1,0:T(8,128)S(1)}, u32[]{:S(2)}, u32[]{:S(2)}) collective-permute-start(f32[1,32,128]{2,1,0:T(8,128)S(1)} %get-tuple-element.139), channel_id=1, source_target_pairs={{4,0},{8,4},{12,8},{16,12},{20,16},{24,20},{28,24},{5,1},{9,5},{13... | collective-permute-start | bytes 49160 | tf_op jit(solution)/shard_map/while/body/eval_jaxpr/ppermute | solution.py:29
  45.7 4.2 collective-permute-start.2
  48.6 4.0 collective-permute-start.3
  53.1 4.4 collective-permute-start
  56.1 5.6 %collective-permute-start.1 = (f32[1,32,128]{2,1,0:T(8,128)S(1)}, f32[1,32,128]{2,1,0:T(8,128)S(1)}, u32[]{:S(2)}, u32[]{:S(2)}) collective-permute-start(f32[1,32,128]{2,1,0:T(8,128)S(1)} %get-tuple-element.139), channel_id=1, source_target_pairs={{4,0},{8,4},{12,8},{16,12},{20,16},{24,20},{28,24},{5,1},{9,5},{13... | collective-permute-start | bytes 49160 | tf_op jit(solution)/shard_map/while/body/eval_jaxpr/ppermute | solution.py:29
  61.7 4.5 collective-permute-start.2
  69.1 6.3 %collective-permute-start = (f32[1,32,128]{2,1,0:T(8,128)S(1)}, f32[1,32,128]{2,1,0:T(8,128)S(1)}, u32[]{:S(2)}, u32[]{:S(2)}) collective-permute-start(f32[1,32,128]{2,1,0:T(8,128)S(1)} %get-tuple-element.138), channel_id=1, source_target_pairs={{0,4},{4,8},{8,12},{12,16},{16,20},{20,24},{24,28},{1,5},{5,9},{9,... | collective-permute-start | bytes 49160 | tf_op jit(solution)/shard_map/while/body/eval_jaxpr/ppermute | solution.py:27
  73.9 5.6 %collective-permute-start.1 = (f32[1,32,128]{2,1,0:T(8,128)S(1)}, f32[1,32,128]{2,1,0:T(8,128)S(1)}, u32[]{:S(2)}, u32[]{:S(2)}) collective-permute-start(f32[1,32,128]{2,1,0:T(8,128)S(1)} %get-tuple-element.139), channel_id=1, source_target_pairs={{4,0},{8,4},{12,8},{16,12},{20,16},{24,20},{28,24},{5,1},{9,5},{13... | collective-permute-start | bytes 49160 | tf_op jit(solution)/shard_map/while/body/eval_jaxpr/ppermute | solution.py:29
  79.6 4.2 collective-permute-start.2
  82.5 4.0 collective-permute-start.3
  88.2 242.0 %all-reduce.9.cloned.1.call-start = ((), (), s32[]{:S(2)}) async-start(), calls=%async_computation.1 | async-start | bytes 131072 | tf_op jit(solution)/shard_map/psum | solution.py:80
  208.2 197.8 %all-reduce.13.cloned.1.call-start = ((), (), s32[]{:S(2)}) async-start(), calls=%async_computation.3 | async-start | bytes 262144 | tf_op jit(solution)/shard_map/psum | solution.py:90
  355.2 5.9 %collective-permute-start.6 = (f32[1,32,128]{2,1,0:T(8,128)S(1)}, f32[1,32,128]{2,1,0:T(8,128)S(1)}, u32[]{:S(2)}, u32[]{:S(2)}) collective-permute-start(f32[1,32,128]{2,1,0:T(8,128)S(1)} %get-tuple-element.82), channel_id=1, source_target_pairs={{4,0},{8,4},{12,8},{16,12},{20,16},{24,20},{28,24},{5,1},{9,5},{13... | collective-permute-start | bytes 49160 | tf_op jit(solution)/shard_map/ppermute | solution.py:29
  356.5 6.0 %collective-permute-start.7 = (f32[1,32,128]{2,1,0:T(8,128)S(1)}, f32[1,32,128]{2,1,0:T(8,128)S(1)}, u32[]{:S(2)}, u32[]{:S(2)}) collective-permute-start(f32[1,32,128]{2,1,0:T(8,128)S(1)} %get-tuple-element.81), channel_id=1, source_target_pairs={{0,4},{4,8},{8,12},{12,16},{16,20},{20,24},{24,28},{1,5},{5,9},{9,... | collective-permute-start | bytes 49160 | tf_op jit(solution)/shard_map/ppermute | solution.py:27
  362.5 5.7 %collective-permute-start.8 = (f32[18,1,128]{2,1,0:T(1,128)S(1)}, f32[18,1,128]{2,1,0:T(1,128)S(1)}, u32[]{:S(2)}, u32[]{:S(2)}) collective-permute-start(f32[18,1,128]{2,1,0:T(1,128)S(1)} %get-tuple-element.79), channel_id=1, source_target_pairs={{1,0},{2,1},{3,2},{5,4},{6,5},{7,6},{9,8},{10,9},{11,10},{13,12},{... | collective-permute-start | bytes 27656 | tf_op jit(solution)/shard_map/ppermute | solution.py:29
  363.8 4.4 collective-permute-start.9
  369.8 109.8 %all-reduce.11.cloned.1.call-start = ((), (), s32[]{:S(2)}) async-start(), calls=%async_computation.2 | async-start | bytes 262144 | tf_op jit(solution)/shard_map/psum | solution.py:89
  (10 other events, 96.1 us)
Sparse Core Ops, SparseCore 0:
  88.3 117.3 all-reduce.6
  211.8 118.3 all-reduce.8
  369.9 35.9 all-reduce.12
  409.7 69.8 all-reduce.10
